TPU v7x, 512 devices: a whole 4x8x8 slice. The times are simulated.
512 devices in a mesh: grp: 16 (over z, core), tok: 32 (over y, x).
Axes of the slice: x: 4, y: 8, z: 8, core: 2. Of those that a mesh axis runs over, the one named last changes fastest.
Arguments:
- patches: bfloat16 [32, 256, 1664], P('tok', 'grp'), may hold values from -54 to 54
- segment_ids: int32 [32, 256], P('tok'), may hold values from 0 to 32, as said below
- padding: int32 [32, 256], P('tok'), may hold values from 0 to 1, as said below
- request_owner: int32 [32, 32], P('tok'), may hold values from 0 to 31, as said below
- first_gain: float32 [1664], replicated, may hold values from 0.5 to 1.5
- first_shift: float32 [1664], replicated, may hold values from -3 to 3
- input_weight: bfloat16 [1664, 16, 312], P(None, 'grp'), may hold values from -0.15625 to 0.15625
- input_shift: float32 [16, 312], P('grp'), may hold values from -40 to 40
- output_weight: bfloat16 [16, 104, 1664], P('grp'), may hold values from -0.15625 to 0.15625
- output_shift: float32 [1664], replicated, may hold values from -3 to 3
- second_gain: float32 [1664], replicated, may hold values from 0.5 to 1.5
- second_shift: float32 [1664], replicated, may hold values from -3 to 3
- up_weight: bfloat16 [1664, 4096], P(None, 'grp'), may hold values from -0.15625 to 0.15625
- up_shift: float32 [4096], P('grp'), may hold values from -3 to 3
- down_weight: bfloat16 [4096, 1664], P('grp'), may hold values from -0.09375 to 0.09375
- down_shift: float32 [1664], replicated, may hold values from -3 to 3
- merge_weight: bfloat16 [6656, 1664], P(None, 'grp'), may hold values from -0.078125 to 0.078125
- merge_shift: float32 [1664], P('grp'), may hold values from -3 to 3
Outputs:
- routed: bfloat16 [32, 32, 8, 1664], P('tok', None, None, 'grp')
Inputs may be any that keep to these rules, and one draw needn't show every extreme that they name: `segment_ids`: patches come in aligned runs of four with one id (a 2x2 window); ids never fall along a group; an image spans 1 to 8 windows; every group holds an image of exactly 8 windows; padding stands at the end of a group and carries the id 32. `padding`: 0 exactly where segment_ids is 32. `request_owner`: every row is a permutation of 0 to 31; in every draw one owner receives an image of 8 windows from every group.
All inputs are finite; a program needn't handle non-finite values.
Results may differ from a plain program's by a relative error of at most 0.02.
The roundings to bfloat16 on the way count: a program that leaves them out, or rounds other values in their place, can miss the bound.
Values may be sent and summed in bfloat16 or wider, within the bound.
No kernel may reach another device: no remote copies, remote signals or barrier semaphores. Data moves between devices by JAX's collectives and lax.ppermute only.
A program may use at most 64 MiB of HBM per device.

v0:
```python
import jax
import jax.numpy as jnp
from jax import lax
from jax.sharding import PartitionSpec as P

CAP = 8
epsilon = 1e-06


def normalize(stream, factor, adjust):
    average = jnp.mean(stream, axis=-1, keepdims=True)
    centered = stream - average
    variance = jnp.mean(centered * centered, axis=-1, keepdims=True)
    return centered * lax.rsqrt(variance + epsilon) * factor + adjust


def attention_mask(segments, live_rows):
    count = segments.shape[0]
    same_image = segments[:, None] == segments[None, :]
    allowed = jnp.logical_and(same_image, live_rows[None, :] == 1)
    diagonal = jnp.arange(count)[:, None] == jnp.arange(count)[None, :]
    return jnp.logical_or(allowed, diagonal)


def softmax_rows(scores, allowed):
    masked = jnp.where(allowed, scores, -jnp.inf)
    row_max = jnp.max(masked, axis=-1, keepdims=True)
    powered = jnp.where(allowed, jnp.exp(masked - row_max), 0.0)
    return powered / jnp.sum(powered, axis=-1, keepdims=True)


def attend(projected, segments, live_rows, head_dim):
    queries = projected[:, :, :head_dim]
    key_rows = projected[:, :, head_dim : 2 * head_dim]
    value_rows = projected[:, :, 2 * head_dim :]
    scores = jnp.einsum(
        "qhe,khe->hqk", queries, key_rows, preferred_element_type=jnp.float32
    ) * head_dim ** (-0.5)
    probabilities = lax.optimization_barrier(
        softmax_rows(scores, attention_mask(segments, live_rows)[None]).astype(jnp.bfloat16)
    )
    return jnp.einsum(
        "hqk,khe->qhe", probabilities, value_rows, preferred_element_type=jnp.float32
    ).astype(jnp.bfloat16)


def summed_apart(terms):
    shards = lax.psum(1, "grp")
    rows = terms.shape[0] // shards
    pieces = lax.all_to_all(terms.reshape(shards, rows, terms.shape[1]), "grp", 0, 0, tiled=False)
    return jnp.sum(pieces.astype(jnp.float32), axis=0)


def routed_rows(merged, segments, live_rows, owners):
    window_segments = segments[::4]
    window_live = live_rows[::4]
    window_count = window_segments.shape[0]
    places = jnp.arange(window_count)
    earlier = jnp.logical_and(
        window_segments[None, :] == window_segments[:, None], places[None, :] < places[:, None]
    )
    slot_index = jnp.sum(earlier.astype(jnp.int32), axis=1)
    groups = owners.shape[0]
    matched = (jnp.arange(groups)[None, :] == window_segments[:, None]).astype(jnp.int32)
    owner_of = jnp.sum(matched * owners[None, :], axis=1)
    target = owner_of * CAP + slot_index
    one_hot = jnp.logical_and(
        target[:, None] == jnp.arange(groups * CAP)[None, :], window_live[:, None] == 1
    )
    outgoing = jnp.einsum(
        "wc,wd->cd", one_hot.astype(jnp.bfloat16), merged, preferred_element_type=jnp.float32
    )
    return outgoing.astype(jnp.bfloat16).reshape(groups, CAP, merged.shape[1])


def on_device(
    patches,
    segment_ids,
    padding,
    request_owner,
    first_gain,
    first_shift,
    input_weight,
    input_shift,
    output_weight,
    output_shift,
    second_gain,
    second_shift,
    up_weight,
    up_shift,
    down_weight,
    down_shift,
    merge_weight,
    merge_shift,
):
    row_count = patches.shape[1]
    model_width = patches.shape[2]
    head_dim = input_weight.shape[2] // 3
    segments = segment_ids[0]
    live_rows = padding[0]
    stream = patches[0]
    gathered = lax.all_gather(stream, "grp", axis=0, tiled=True)
    normed = normalize(gathered.astype(jnp.float32), first_gain, first_shift).astype(jnp.bfloat16)
    lifted = jnp.einsum("sd,dhe->she", normed, input_weight, preferred_element_type=jnp.float32)
    projected = (lifted + input_shift[None]).astype(jnp.bfloat16)
    mixed = attend(projected, segments, live_rows, head_dim)
    block = lax.optimization_barrier(mixed)
    attended = summed_apart(
        jnp.einsum("qhe,hed->qd", block, output_weight, preferred_element_type=jnp.float32).astype(
            jnp.bfloat16
        )
    )
    residual = (stream.astype(jnp.float32) + attended + output_shift).astype(jnp.bfloat16)
    normed_again = normalize(residual.astype(jnp.float32), second_gain, second_shift).astype(
        jnp.bfloat16
    )
    lifted = (
        jnp.dot(
            lax.all_gather(normed_again, "grp", axis=0, tiled=True),
            up_weight,
            preferred_element_type=jnp.float32,
        )
        + up_shift
    )
    activated = jax.nn.gelu(lifted, approximate=False).astype(jnp.bfloat16)
    block = lax.optimization_barrier(activated)
    fed = summed_apart(
        jnp.dot(block, down_weight, preferred_element_type=jnp.float32).astype(jnp.bfloat16)
    )
    layer_out = (residual.astype(jnp.float32) + fed + down_shift).astype(jnp.bfloat16)
    windows = layer_out.reshape(row_count // 4, 4 * model_width)
    merged = (
        jnp.dot(
            lax.all_gather(windows, "grp", axis=0, tiled=True),
            merge_weight,
            preferred_element_type=jnp.float32,
        )
        + merge_shift
    ).astype(jnp.bfloat16)
    outgoing = routed_rows(merged, segments, live_rows, request_owner[0])
    delivered = lax.all_to_all(outgoing, "tok", split_axis=0, concat_axis=0, tiled=True)
    return delivered[None]


def solution(mesh):
    return jax.shard_map(
        on_device,
        mesh=mesh,
        in_specs=(
            P("tok", "grp", None),
            P("tok", None),
            P("tok", None),
            P("tok", None),
            P(),
            P(),
            P(None, "grp", None),
            P("grp", None),
            P("grp", None, None),
            P(),
            P(),
            P(),
            P(None, "grp"),
            P("grp"),
            P("grp", None),
            P(),
            P(None, "grp"),
            P("grp"),
        ),
        out_specs=P("tok", None, None, "grp"),
        check_vma=False,
    )
```

profile of v0, /device:TPU:1, one launch (start us, length us, event | category | flops | bytes accessed | tf_op | source)
XLA Modules:
  0.0 143.6 jit_solution(7038068006779687679)
XLA Ops:
  0.0 0.0 copy-start
  0.0 0.0 copy-start.14
  0.0 0.0 copy-start.13
  0.0 27.2 %all-gather = bf16[1,256,1664]{2,1,0:T(8,128)(2,1)S(1)} all-gather(bf16[1,16,1664]{2,1,0:T(8,128)(2,1)} %param.18), channel_id=2, replica_groups=mesh['grp'=16,'tok'=32] {'grp'}, dimensions={1}, use_global_device_ids=true | all-gather | bytes 905216 | tf_op jit(solution)/shard_map/all_gather | solution.py:102
  27.2 0.2 convert_reduce_fusion
  27.5 0.4 fusion.3
  27.8 0.0 copy-done.16
  27.9 0.0 copy-done.14
  27.9 0.0 copy-done.13
  27.9 0.0 copy-done.11
  27.9 0.0 copy-start.5
  27.9 0.7 fusion.9
  28.6 0.0 copy-start.3
  28.6 0.3 fusion.50
  28.9 0.2 fusion.30
  29.1 0.1 fusion.32
  29.2 0.2 fusion.10
  29.4 0.2 copy-done.3
  29.6 0.4 convolution_convert_fusion.1
  30.0 0.0 copy-start.2
  30.1 0.0 copy-start.4
  30.1 0.0 copy-start.7
  30.1 0.0 copy-start.8
  30.1 27.0 %all_to_all.15 = bf16[16,16,1664]{2,1,0:T(8,128)(2,1)S(1)} all-to-all(bf16[16,16,1664]{2,1,0:T(8,128)(2,1)S(1)} %bitcast.72), channel_id=1, replica_groups=mesh['grp'=16,'tok'=32] {'grp'}, dimensions={0} | all-to-all | bytes 1703936 | tf_op jit(solution)/shard_map/all_to_all | solution.py:50
  57.1 0.1 convert_reduce_fusion.2
  57.3 0.0 copy-done.2
  57.3 0.1 convert_reduce_fusion.3
  57.4 0.2 fusion.35
  57.7 0.1 fusion.38
  57.7 16.8 %all_gather.10 = bf16[256,1664]{1,0:T(8,128)(2,1)S(1)} all-gather(bf16[16,1664]{1,0:T(8,128)(2,1)S(1)} %fusion.38), channel_id=1, replica_groups=mesh['grp'=16,'tok'=32] {'grp'}, dimensions={0}, use_global_device_ids=true | all-gather | bytes 905216 | tf_op jit(solution)/shard_map/all_gather | solution.py:119
  74.6 1.0 fusion.21
  75.6 0.2 copy-done.1
  75.7 1.4 convolution_convert_fusion
  77.1 5.3 %all-to-all-start.1 = ((bf16[16,16,1664]{2,1,0:T(8,128)(2,1)}), bf16[16,16,1664]{2,1,0:T(8,128)(2,1)S(1)}, u32[]{:S(2)}, u32[]{:S(2)}) async-start(bf16[16,16,1664]{2,1,0:T(8,128)(2,1)} %bitcast.17), calls=%async_computation.1 | async-start | bytes 1703936 | tf_op jit(solution)/shard_map/all_to_all | solution.py:50
  82.4 0.2 slice.15
  82.7 0.2 slice.16
  82.8 0.2 convert_reduce_fusion.4
  83.0 0.1 select_reduce_fusion
  83.2 23.3 %all-to-all-done.1 = bf16[16,16,1664]{2,1,0:T(8,128)(2,1)S(1)} async-done(((bf16[16,16,1664]{2,1,0:T(8,128)(2,1)}), bf16[16,16,1664]{2,1,0:T(8,128)(2,1)S(1)}, u32[]{:S(2)}, u32[]{:S(2)}) %all-to-all-start.1) | async-done | bytes 852000 | tf_op jit(solution)/shard_map/all_to_all | solution.py:50
  106.4 0.1 convert_reduce_fusion.1
  106.6 0.1 fusion.43
  106.7 0.0 copy-start.10
  106.7 16.8 %all-gather.1 = bf16[16,4,6656]{2,1,0:T(4,128)(2,1)S(1)} all-gather(bf16[1,4,6656]{2,1,0:T(4,128)(2,1)S(1)} %fusion.43), channel_id=1, replica_groups=mesh['grp'=16,'tok'=32] {'grp'}, dimensions={0}, use_global_device_ids=true | all-gather | bytes 905216 | tf_op jit(solution)/shard_map/all_gather | solution.py:134
  123.5 0.2 reshape.122
  123.7 0.8 convolution_convert_fusion.2
  124.5 0.1 copy.26
  124.7 18.3 %all_to_all.16 = bf16[32,8,104]{2,1,0:T(8,128)(2,1)S(1)} all-to-all(bf16[32,8,104]{2,1,0:T(8,128)(2,1)S(1)} %bitcast.73), channel_id=1, replica_groups=mesh['grp'=16,'tok'=32] {'tok'}, dimensions={0} | all-to-all | bytes 106496 | tf_op jit(solution)/shard_map/all_to_all | solution.py:141
  143.0 0.6 copy.29
  (34 shorter events, 0.3 us)
Async XLA Ops:
  0.0 123.7 %copy-start = (bf16[6656,104]{0,1:T(8,128)(2,1)S(1)}, bf16[6656,104]{0,1:T(8,128)(2,1)}, u32[]{:S(2)}) copy-start(bf16[6656,104]{0,1:T(8,128)(2,1)} %param.34) | copy-start | bytes 4153348
  0.0 27.8 %copy-start.16 = (s32[1,256]{1,0:T(1,128)S(1)}, s32[1,256]{1,0:T(1,128)}, u32[]{:S(2)}) copy-start(s32[1,256]{1,0:T(1,128)} %param.20) | copy-start | bytes 3076
  0.0 27.9 %copy-start.9 = (f32[1,312]{1,0:T(1,128)S(1)}, f32[1,312]{1,0:T(1,128)}, u32[]{:S(2)}) copy-start(f32[1,312]{1,0:T(1,128)} %param.25) | copy-start | bytes 3748
  0.0 27.9 %copy-start.14 = (f32[1664]{0:T(1024)S(1)}, f32[1664]{0:T(1024)}, u32[]{:S(2)}) copy-start(f32[1664]{0:T(1024)} %param.22) | copy-start | bytes 19972
  0.0 27.9 %copy-start.13 = (f32[1664]{0:T(1024)S(1)}, f32[1664]{0:T(1024)}, u32[]{:S(2)}) copy-start(f32[1664]{0:T(1024)} %param.23) | copy-start | bytes 19972
  0.0 27.9 %copy-start.11 = (bf16[1664,1,312]{0,2,1:T(8,128)(2,1)S(1)}, bf16[1664,1,312]{0,2,1:T(8,128)(2,1)}, u32[]{:S(2)}) copy-start(bf16[1664,1,312]{0,2,1:T(8,128)(2,1)} %param.24) | copy-start | bytes 3115012
  27.9 0.7 copy-start.5
  28.6 1.0 copy-start.3
  30.0 27.2 %copy-start.2 = (bf16[1,16,1664]{2,1,0:T(8,128)(2,1)S(1)}, bf16[1,16,1664]{2,1,0:T(8,128)(2,1)}, u32[]{:S(2)}) copy-start(bf16[1,16,1664]{2,1,0:T(8,128)(2,1)} %param.18) | copy-start | bytes 159748
  30.1 27.2 %copy-start.4 = (f32[1664]{0:T(1024)S(1)}, f32[1664]{0:T(1024)}, u32[]{:S(2)}) copy-start(f32[1664]{0:T(1024)} %param.27) | copy-start | bytes 19972
  30.1 27.6 %copy-start.7 = (f32[1664]{0:T(1024)S(1)}, f32[1664]{0:T(1024)}, u32[]{:S(2)}) copy-start(f32[1664]{0:T(1024)} %param.29) | copy-start | bytes 19972
  30.1 27.6 %copy-start.8 = (f32[1664]{0:T(1024)S(1)}, f32[1664]{0:T(1024)}, u32[]{:S(2)}) copy-start(f32[1664]{0:T(1024)} %param.28) | copy-start | bytes 19972
  57.1 17.4 %copy-start.12 = (bf16[1664,256]{1,0:T(8,128)(2,1)S(1)}, bf16[1664,256]{1,0:T(8,128)(2,1)}, u32[]{:S(2)}) copy-start(bf16[1664,256]{1,0:T(8,128)(2,1)} %param.30) | copy-start | bytes 2555908
  57.1 17.4 %copy-start.15 = (f32[256]{0:T(256)S(1)}, f32[256]{0:T(256)}, u32[]{:S(2)}) copy-start(f32[256]{0:T(256)} %param.31) | copy-start | bytes 3076
  74.6 1.2 copy-start.1
  77.1 5.6 %copy-start.6 = (f32[1664]{0:T(1024)S(1)}, f32[1664]{0:T(1024)}, u32[]{:S(2)}) copy-start(f32[1664]{0:T(1024)} %param.33) | copy-start | bytes 19972
  77.1 5.9 %copy-start.17 = (s32[1,32]{1,0:T(1,128)S(1)}, s32[1,32]{1,0:T(1,128)}, u32[]{:S(2)}) copy-start(s32[1,32]{1,0:T(1,128)} %param.21) | copy-start | bytes 388
  77.1 29.4 %all-to-all-start.1 = ((bf16[16,16,1664]{2,1,0:T(8,128)(2,1)}), bf16[16,16,1664]{2,1,0:T(8,128)(2,1)S(1)}, u32[]{:S(2)}, u32[]{:S(2)}) async-start(bf16[16,16,1664]{2,1,0:T(8,128)(2,1)} %bitcast.17), calls=%async_computation.1 | async-start | bytes 1703936 | tf_op jit(solution)/shard_map/all_to_all | solution.py:50
  106.7 17.0 %copy-start.10 = (f32[104]{0:T(128)S(1)}, f32[104]{0:T(128)}, u32[]{:S(2)}) copy-start(f32[104]{0:T(128)} %param.35) | copy-start | bytes 1252
where the time goes:
time: 144 us
  blocking collectives  106 us (74%)
  waiting for transfers between devices  23.3 us (16%)
  starting transfers between devices  5.33 us (4%)
  matrix products  4.68 us (3%)
  other arithmetic  1.96 us (1%)
  local copies, waits for them, and re-layouts  1.85 us (1%)
    all_gather x1, blocking collectives, on_device(): gathered = lax.all_gather(stream, 'grp', axis=0, tiled=True)  27.2 us
    all_to_all x1, blocking collectives, summed_apart(): lax.all_to_all(terms.reshape(shards, rows, terms.shape[1]), 'grp', 0, 0,...  27 us
    all_to_all x1, waiting for transfers between devices, summed_apart(): lax.all_to_all(terms.reshape(shards, rows, terms.shape[1]), 'grp', 0, 0,...  23.3 us
    all_to_all x1, blocking collectives, on_device(): lax.all_to_all(outgoing, 'tok', split_axis=0, concat_axis=0, tiled=True)  18.3 us
    all_gather x1, blocking collectives, on_device(): lax.all_gather(windows, 'grp', axis=0, tiled=True)  16.8 us
    all_gather x1, blocking collectives, on_device(): lax.all_gather(normed_again, 'grp', axis=0, tiled=True)  16.8 us
    all_to_all x1, starting transfers between devices, summed_apart(): lax.all_to_all(terms.reshape(shards, rows, terms.shape[1]), 'grp', 0, 0,...  5.33 us
  transfers between devices with their start and end apart: 1, of which 1 were waited for; matrix products, arithmetic and copies ran while one was open for 0% of the time, Pallas kernels for 0%

commit v1 on v0

--- a/solution.py
+++ b/solution.py
@@ -1,3 +1,4 @@
+import functools
 import jax
 import jax.numpy as jnp
 from jax import lax
@@ -5,6 +6,15 @@
 
 CAP = 8
 epsilon = 1e-06
+
+
+def values_match(local_array, mesh_dim, dim_i):
+    kept_arr = jnp.stack([local_array for _ in range(lax.psum(1, mesh_dim))])
+    outer = lax.all_to_all(kept_arr, mesh_dim, 0, 0)
+    return jnp.concatenate(outer, axis=dim_i)
+
+
+close_trails = functools.partial(values_match, mesh_dim="grp", dim_i=0)
 
 
 def normalize(stream, factor, adjust):
@@ -130,11 +140,7 @@
     layer_out = (residual.astype(jnp.float32) + fed + down_shift).astype(jnp.bfloat16)
     windows = layer_out.reshape(row_count // 4, 4 * model_width)
     merged = (
-        jnp.dot(
-            lax.all_gather(windows, "grp", axis=0, tiled=True),
-            merge_weight,
-            preferred_element_type=jnp.float32,
-        )
+        jnp.dot(close_trails(windows), merge_weight, preferred_element_type=jnp.float32)
         + merge_shift
     ).astype(jnp.bfloat16)
     outgoing = routed_rows(merged, segments, live_rows, request_owner[0])

time: 144 us -> 156 us (1.083)
  waiting for transfers between devices: 23.3 us -> 46.9 us
  blocking collectives: 106 us -> 89.4 us
  starting transfers between devices: 5.33 us -> 8.98 us
    all_to_all x0 -> x1, waiting for transfers between devices: none -> 23 us  [values_match(): outer = lax.all_to_all(kept_arr, mesh_dim, 0, 0)]
    all_gather x1 -> x0, blocking collectives: 16.8 us -> none  [on_device(): lax.all_gather(windows, 'grp', axis=0, tiled=True)]
    all_to_all x0 -> x1, starting transfers between devices: none -> 3.65 us  [values_match(): outer = lax.all_to_all(kept_arr, mesh_dim, 0, 0)]
  transfers between devices with their start and end apart: 1 -> 2, of which waited for: 1 -> 2; matrix products, arithmetic and copies ran while one was open for 0% -> 0% of each run, Pallas kernels for 0% -> 0%
where the time goes in v1:
time: 156 us; the launch traced here: 155 us
  blocking collectives  89.4 us (57%)
  waiting for transfers between devices  46.9 us (30%)
  starting transfers between devices  8.98 us (6%)
  matrix products  4.68 us (3%)
  local copies, waits for them, and re-layouts  2.99 us (2%)
  other arithmetic  1.95 us (1%)
    all_gather x1, blocking collectives, on_device(): gathered = lax.all_gather(stream, 'grp', axis=0, tiled=True)  27.2 us
    all_to_all x1, blocking collectives, summed_apart(): lax.all_to_all(terms.reshape(shards, rows, terms.shape[1]), 'grp', 0, 0,...  27 us
    all_to_all x1, waiting for transfers between devices, summed_apart(): lax.all_to_all(terms.reshape(shards, rows, terms.shape[1]), 'grp', 0, 0,...  23.9 us
    all_to_all x1, waiting for transfers between devices, values_match(): outer = lax.all_to_all(kept_arr, mesh_dim, 0, 0)  23 us
    all_to_all x1, blocking collectives, on_device(): lax.all_to_all(outgoing, 'tok', split_axis=0, concat_axis=0, tiled=True)  18.3 us
    all_gather x1, blocking collectives, on_device(): lax.all_gather(normed_again, 'grp', axis=0, tiled=True)  16.8 us
    all_to_all x1, starting transfers between devices, summed_apart(): lax.all_to_all(terms.reshape(shards, rows, terms.shape[1]), 'grp', 0, 0,...  5.33 us
    all_to_all x1, starting transfers between devices, values_match(): outer = lax.all_to_all(kept_arr, mesh_dim, 0, 0)  3.65 us
  transfers between devices with their start and end apart: 2, of which 2 were waited for; matrix products, arithmetic and copies ran while one was open for 0% of the time, Pallas kernels for 0%

profile of v1, /device:TPU:1, one launch (start us, length us, event | category | flops | bytes accessed | tf_op | source)
XLA Modules:
  0.0 155.2 jit_solution(5410796431067598895)
XLA Ops:
  0.0 27.2 %all-gather = bf16[1,256,1664]{2,1,0:T(8,128)(2,1)S(1)} all-gather(bf16[1,16,1664]{2,1,0:T(8,128)(2,1)} %param.18), channel_id=2, replica_groups=mesh['grp'=16,'tok'=32] {'grp'}, dimensions={1}, use_global_device_ids=true | all-gather | bytes 905216 | tf_op jit(solution)/shard_map/all_gather | solution.py:112
  27.2 0.2 convert_reduce_fusion
  27.5 0.4 fusion.3
  27.8 0.0 copy-done.16
  27.9 0.0 copy-done.14
  27.9 0.0 copy-done.13
  27.9 0.0 copy-done.11
  27.9 0.0 copy-start.5
  27.9 0.7 fusion.9
  28.6 0.0 copy-start.3
  28.6 0.0 copy-done.5
  28.6 0.3 fusion.49
  28.9 0.2 fusion.30
  29.1 0.1 fusion.32
  29.2 0.2 fusion.10
  29.4 0.2 copy-done.3
  29.6 0.4 convolution_convert_fusion.1
  30.0 0.0 copy-start.2
  30.1 0.0 copy-start.4
  30.1 0.0 copy-start.7
  30.1 0.0 copy-start.8
  30.1 27.0 %all_to_all.20 = bf16[16,16,1664]{2,1,0:T(8,128)(2,1)S(1)} all-to-all(bf16[16,16,1664]{2,1,0:T(8,128)(2,1)S(1)} %bitcast.70), channel_id=1, replica_groups=mesh['grp'=16,'tok'=32] {'grp'}, dimensions={0} | all-to-all | bytes 1703936 | tf_op jit(solution)/shard_map/all_to_all | solution.py:60
  57.1 0.1 convert_reduce_fusion.2
  57.3 0.1 convert_reduce_fusion.3
  57.4 0.2 fusion.35
  57.6 0.1 fusion.38
  57.7 16.8 %all_gather.7 = bf16[256,1664]{1,0:T(8,128)(2,1)S(1)} all-gather(bf16[16,1664]{1,0:T(8,128)(2,1)S(1)} %fusion.38), channel_id=1, replica_groups=mesh['grp'=16,'tok'=32] {'grp'}, dimensions={0}, use_global_device_ids=true | all-gather | bytes 905216 | tf_op jit(solution)/shard_map/all_gather | solution.py:129
  74.6 1.0 fusion.21
  75.6 0.2 copy-done.1
  75.7 1.3 convolution_convert_fusion
  77.1 5.3 %all-to-all-start.1 = ((bf16[16,16,1664]{2,1,0:T(8,128)(2,1)}), bf16[16,16,1664]{2,1,0:T(8,128)(2,1)S(1)}, u32[]{:S(2)}, u32[]{:S(2)}) async-start(bf16[16,16,1664]{2,1,0:T(8,128)(2,1)} %bitcast.17), calls=%async_computation.1 | async-start | bytes 1703936 | tf_op jit(solution)/shard_map/all_to_all | solution.py:60
  82.5 0.0 copy-done.6
  82.6 23.9 %all-to-all-done.1 = bf16[16,16,1664]{2,1,0:T(8,128)(2,1)S(1)} async-done(((bf16[16,16,1664]{2,1,0:T(8,128)(2,1)}), bf16[16,16,1664]{2,1,0:T(8,128)(2,1)S(1)}, u32[]{:S(2)}, u32[]{:S(2)}) %all-to-all-start.1) | async-done | bytes 852000 | tf_op jit(solution)/shard_map/all_to_all | solution.py:60
  106.4 0.1 convert_reduce_fusion.1
  106.6 0.1 add_convert_fusion
  106.7 0.0 copy-start.17
  106.7 1.1 stack.3
  107.8 3.7 %all-to-all-start.2 = ((bf16[16,4,6656]{2,1,0:T(4,128)(2,1)}), bf16[16,4,6656]{2,1,0:T(4,128)(2,1)S(1)}, u32[]{:S(2)}, u32[]{:S(2)}) async-start(bf16[16,4,6656]{2,1,0:T(4,128)(2,1)} %stack.3), calls=%async_computation.2 | async-start | bytes 1703936 | tf_op jit(solution)/shard_map/all_to_all | solution.py:13
  111.5 0.2 slice.15
  111.6 0.2 slice.16
  111.8 0.2 convert_reduce_fusion.4
  112.0 0.1 select_reduce_fusion
  112.1 23.0 %all-to-all-done.2 = bf16[16,4,6656]{2,1,0:T(4,128)(2,1)S(1)} async-done(((bf16[16,4,6656]{2,1,0:T(4,128)(2,1)}), bf16[16,4,6656]{2,1,0:T(4,128)(2,1)S(1)}, u32[]{:S(2)}, u32[]{:S(2)}) %all-to-all-start.2) | async-done | bytes 852000 | tf_op jit(solution)/shard_map/all_to_all | solution.py:13
  135.1 0.2 reshape.122
  135.3 0.8 convolution_convert_fusion.2
  136.1 0.1 copy.24
  136.3 18.3 %all_to_all.21 = bf16[32,8,104]{2,1,0:T(8,128)(2,1)S(1)} all-to-all(bf16[32,8,104]{2,1,0:T(8,128)(2,1)S(1)} %bitcast.71), channel_id=1, replica_groups=mesh['grp'=16,'tok'=32] {'tok'}, dimensions={0} | all-to-all | bytes 106496 | tf_op jit(solution)/shard_map/all_to_all | solution.py:147
  154.5 0.6 copy.27
  (36 shorter events, 0.3 us)
Async XLA Ops:
  0.0 135.3 %copy-start = (bf16[6656,104]{0,1:T(8,128)(2,1)S(1)}, bf16[6656,104]{0,1:T(8,128)(2,1)}, u32[]{:S(2)}) copy-start(bf16[6656,104]{0,1:T(8,128)(2,1)} %param.34) | copy-start | bytes 4153348
  0.0 27.8 %copy-start.16 = (s32[1,256]{1,0:T(1,128)S(1)}, s32[1,256]{1,0:T(1,128)}, u32[]{:S(2)}) copy-start(s32[1,256]{1,0:T(1,128)} %param.20) | copy-start | bytes 3076
  0.0 27.9 %copy-start.9 = (f32[1,312]{1,0:T(1,128)S(1)}, f32[1,312]{1,0:T(1,128)}, u32[]{:S(2)}) copy-start(f32[1,312]{1,0:T(1,128)} %param.25) | copy-start | bytes 3748
  0.0 27.9 %copy-start.14 = (f32[1664]{0:T(1024)S(1)}, f32[1664]{0:T(1024)}, u32[]{:S(2)}) copy-start(f32[1664]{0:T(1024)} %param.22) | copy-start | bytes 19972
  0.0 27.9 %copy-start.13 = (f32[1664]{0:T(1024)S(1)}, f32[1664]{0:T(1024)}, u32[]{:S(2)}) copy-start(f32[1664]{0:T(1024)} %param.23) | copy-start | bytes 19972
  0.0 27.9 %copy-start.11 = (bf16[1664,1,312]{0,2,1:T(8,128)(2,1)S(1)}, bf16[1664,1,312]{0,2,1:T(8,128)(2,1)}, u32[]{:S(2)}) copy-start(bf16[1664,1,312]{0,2,1:T(8,128)(2,1)} %param.24) | copy-start | bytes 3115012
  27.9 0.7 copy-start.5
  28.6 1.0 copy-start.3
  30.0 27.2 %copy-start.2 = (bf16[1,16,1664]{2,1,0:T(8,128)(2,1)S(1)}, bf16[1,16,1664]{2,1,0:T(8,128)(2,1)}, u32[]{:S(2)}) copy-start(bf16[1,16,1664]{2,1,0:T(8,128)(2,1)} %param.18) | copy-start | bytes 159748
  30.1 27.2 %copy-start.4 = (f32[1664]{0:T(1024)S(1)}, f32[1664]{0:T(1024)}, u32[]{:S(2)}) copy-start(f32[1664]{0:T(1024)} %param.27) | copy-start | bytes 19972
  30.1 27.6 %copy-start.7 = (f32[1664]{0:T(1024)S(1)}, f32[1664]{0:T(1024)}, u32[]{:S(2)}) copy-start(f32[1664]{0:T(1024)} %param.29) | copy-start | bytes 19972
  30.1 27.6 %copy-start.8 = (f32[1664]{0:T(1024)S(1)}, f32[1664]{0:T(1024)}, u32[]{:S(2)}) copy-start(f32[1664]{0:T(1024)} %param.28) | copy-start | bytes 19972
  57.1 17.4 %copy-start.12 = (bf16[1664,256]{1,0:T(8,128)(2,1)S(1)}, bf16[1664,256]{1,0:T(8,128)(2,1)}, u32[]{:S(2)}) copy-start(bf16[1664,256]{1,0:T(8,128)(2,1)} %param.30) | copy-start | bytes 2555908
  57.1 17.4 %copy-start.15 = (f32[256]{0:T(256)S(1)}, f32[256]{0:T(256)}, u32[]{:S(2)}) copy-start(f32[256]{0:T(256)} %param.31) | copy-start | bytes 3076
  74.6 1.2 copy-start.1
  77.1 5.4 %copy-start.6 = (f32[1664]{0:T(1024)S(1)}, f32[1664]{0:T(1024)}, u32[]{:S(2)}) copy-start(f32[1664]{0:T(1024)} %param.33) | copy-start | bytes 19972
  77.1 29.4 %all-to-all-start.1 = ((bf16[16,16,1664]{2,1,0:T(8,128)(2,1)}), bf16[16,16,1664]{2,1,0:T(8,128)(2,1)S(1)}, u32[]{:S(2)}, u32[]{:S(2)}) async-start(bf16[16,16,1664]{2,1,0:T(8,128)(2,1)} %bitcast.17), calls=%async_computation.1 | async-start | bytes 1703936 | tf_op jit(solution)/shard_map/all_to_all | solution.py:60
  106.7 5.3 %copy-start.17 = (s32[1,32]{1,0:T(1,128)S(1)}, s32[1,32]{1,0:T(1,128)}, u32[]{:S(2)}) copy-start(s32[1,32]{1,0:T(1,128)} %param.21) | copy-start | bytes 388
  107.8 27.5 %copy-start.10 = (f32[104]{0:T(128)S(1)}, f32[104]{0:T(128)}, u32[]{:S(2)}) copy-start(f32[104]{0:T(128)} %param.35) | copy-start | bytes 1252
  107.8 27.3 %all-to-all-start.2 = ((bf16[16,4,6656]{2,1,0:T(4,128)(2,1)}), bf16[16,4,6656]{2,1,0:T(4,128)(2,1)S(1)}, u32[]{:S(2)}, u32[]{:S(2)}) async-start(bf16[16,4,6656]{2,1,0:T(4,128)(2,1)} %stack.3), calls=%async_computation.2 | async-start | bytes 1703936 | tf_op jit(solution)/shard_map/all_to_all | solution.py:13
